TPU v7x, 32 devices: a whole 2x2x4 slice. The times are simulated.
32 devices in a mesh: seq: 4 (over y, x), batch: 8 (over z, core).
Axes of the slice: x: 2, y: 2, z: 4, core: 2. Of those that a mesh axis runs over, the one named last changes fastest.
Arguments:
- feats: bfloat16 [768, 4096], P('seq', 'batch'), parts along dimension 1, may hold values from -6 to 6
- qkv_weight: bfloat16 [768, 2304], replicated, may hold values from -0.21875 to 0.21875
- beta_weight: bfloat16 [768, 6], replicated, may hold values from -0.21875 to 0.21875
- beta_bias: float32 [6], replicated, may hold values from -7 to 0.5
- out_gain: float32 [768], replicated, may hold values from 0.1 to 1.9
Outputs:
- mixed: bfloat16 [4096, 768], P(('batch', 'seq')), parts along dimension 0
There are 8 independent parts, one for each index of `batch`. A program takes and returns all parts, laid end to end along the dimension named above; an argument that names none is the same for every part. Nothing has to cross between parts.
All inputs are finite; a program needn't handle non-finite values.
Results may differ from a plain program's by a relative error of at most 0.012.
Values may be sent and summed in bfloat16 or wider, within the bound.
No kernel may reach another device: no remote copies, remote signals or barrier semaphores. Data moves between devices by JAX's collectives and lax.ppermute only.
A program may use at most 64 MiB of HBM per device.

v0:
```python
import jax
import jax.numpy as jnp
from jax import lax
from jax.sharding import PartitionSpec as P

HEADS = 6
HD = 128
GROUP = 64
HIGHEST_ACCURACY = lax.Precision.HIGHEST


def entering(value, axis, join, neutral):
    count, mine = (lax.axis_size(axis), lax.axis_index(axis))
    pieces = jax.tree.map(lambda part: lax.all_gather(part, axis), value)
    running = jax.tree.map(
        lambda part, zero: jnp.full_like(part, 0) + jnp.asarray(zero, part.dtype), value, neutral
    )

    def turn(position, running):
        longer = join(running, jax.tree.map(lambda part: part[position], pieces))
        return jax.tree.map(lambda new, old: jnp.where(position < mine, new, old), longer, running)

    return lax.fori_loop(0, count - 1, turn, running)


def unit_inverse(gram):
    eye_block = jnp.eye(gram.shape[-1], dtype=jnp.float32)
    negated = -jnp.tril(gram, -1)
    inverse = eye_block + negated
    power = negated
    for level in range(5):
        power = jnp.einsum("nhij,nhjk->nhik", power, power, precision=HIGHEST_ACCURACY)
        inverse = inverse + jnp.einsum(
            "nhij,nhjk->nhik", inverse, power, precision=HIGHEST_ACCURACY
        )
    return inverse


def prepare(qkv, beta):
    rows = qkv.shape[0]
    blocks_count = rows // GROUP
    pieces = qkv.astype(jnp.float32).reshape(rows, 3, HEADS, HD)
    query = pieces[:, 0]
    keys = pieces[:, 1]
    values = pieces[:, 2]
    query = query * lax.rsqrt(jnp.sum(query * query, -1, keepdims=True) + 1e-06)
    keys = keys * lax.rsqrt(jnp.sum(keys * keys, -1, keepdims=True) + 1e-06)

    def blocks(arr):
        return arr.reshape(blocks_count, GROUP, HEADS, arr.shape[-1]).transpose(0, 2, 1, 3)

    query = blocks(query)
    keys = blocks(keys)
    values = blocks(values)
    rates = blocks(beta[:, :, None])
    weighted = keys * rates
    gram = jnp.einsum("nhik,nhjk->nhij", weighted, keys, precision=HIGHEST_ACCURACY)
    inverse = unit_inverse(gram)
    right = jnp.concatenate([weighted, values * rates], -1)
    solved = jnp.einsum("nhij,nhjk->nhik", inverse, right, precision=HIGHEST_ACCURACY)
    wfac = solved[..., :HD]
    ufac = solved[..., HD:]
    scores = jnp.tril(jnp.einsum("nhik,nhjk->nhij", query, keys, precision=HIGHEST_ACCURACY))
    return (query, keys, wfac, ufac, scores)


def finish(outputs, out_gain):
    rows = outputs.shape[0] * GROUP
    flat = outputs.transpose(0, 2, 1, 3).reshape(rows, HEADS, HD)
    power = jnp.mean(flat * flat, -1, keepdims=True) + 1e-06
    normed = flat * lax.rsqrt(power) * out_gain.reshape(HEADS, HD)
    return normed.reshape(rows, HEADS * HD).astype(jnp.bfloat16)


def compose(early, late):
    first_move, first_offset = early
    second_move, second_offset = late
    move = jnp.einsum("hij,hjk->hik", second_move, first_move, precision=HIGHEST_ACCURACY)
    offset = (
        jnp.einsum("hij,hjk->hik", second_move, first_offset, precision=HIGHEST_ACCURACY)
        + second_offset
    )
    return (move, offset)


def body(feats, qkv_weight, beta_weight, beta_bias, out_gain):
    local = lax.all_to_all(feats, "seq", split_axis=1, concat_axis=0, tiled=True)
    qkv = lax.dot_general(
        local, qkv_weight, (((0,), (0,)), ((), ())), preferred_element_type=jnp.float32
    ).astype(jnp.bfloat16)
    logits = lax.dot_general(
        local, beta_weight, (((0,), (0,)), ((), ())), preferred_element_type=jnp.float32
    )
    beta = jax.nn.sigmoid(logits + beta_bias)
    query, keys, wfac, ufac, scores = prepare(qkv, beta)
    eye_heads = jnp.broadcast_to(jnp.eye(HD, dtype=jnp.float32), (HEADS, HD, HD))
    empty = jnp.zeros((HEADS, HD, HD), jnp.float32)

    def first_pass(joint_matrix, item):
        query_block, key_block, weight_block, update_block, state_block = item
        held_value = jnp.einsum(
            "rnf,rfw->rnw", weight_block, joint_matrix, precision=HIGHEST_ACCURACY
        )
        carried_state = joint_matrix[..., HD:]
        residual_value = update_block - held_value[..., HD:]
        output_rows = jnp.einsum(
            "rnf,rfw->rnw", query_block, carried_state, precision=HIGHEST_ACCURACY
        ) + jnp.einsum("fco,fop->fcp", state_block, residual_value, precision=HIGHEST_ACCURACY)
        target_value = jnp.concatenate([-held_value[..., :HD], residual_value], -1)
        joint_matrix = joint_matrix + jnp.einsum(
            "mjr,mjz->mrz", key_block, target_value, precision=HIGHEST_ACCURACY
        )
        return (joint_matrix, output_rows)

    joint_start = jnp.concatenate([eye_heads, empty], -1)
    joint_matrix, local_out = lax.scan(first_pass, joint_start, (query, keys, wfac, ufac, scores))
    moves = joint_matrix[..., :HD]
    offsets = joint_matrix[..., HD:]
    prior = entering((moves, offsets), "seq", compose, (eye_heads, empty))
    incoming = prior[1]

    def second_pass(loop_carry, item):
        query_block, key_block, weight_block, state_block = item
        held_value = jnp.einsum(
            "rnf,rfw->rnw", weight_block, loop_carry, precision=HIGHEST_ACCURACY
        )
        output_rows = jnp.einsum(
            "rnf,rfw->rnw", query_block, loop_carry, precision=HIGHEST_ACCURACY
        ) - jnp.einsum("fco,fop->fcp", state_block, held_value, precision=HIGHEST_ACCURACY)
        loop_carry = loop_carry - jnp.einsum(
            "mjr,mjz->mrz", key_block, held_value, precision=HIGHEST_ACCURACY
        )
        return (loop_carry, output_rows)

    final_carry, added_out = lax.scan(second_pass, incoming, (query, keys, wfac, scores))
    return finish(local_out + added_out, out_gain)


def solution(mesh):
    placed = (P("seq", "batch"), P(), P(), P(), P())
    return jax.shard_map(
        body, mesh=mesh, in_specs=placed, out_specs=P(("batch", "seq"), None), check_vma=False
    )
```

profile of v0, /device:TPU:0, one launch (start us, length us, event | category | flops | bytes accessed | tf_op | source)
XLA Modules:
  0.0 174.5 jit_solution(12034097138395976783)
XLA Ops:
  6.5 1.8 %copy_bitcast_fusion = bf16[192,4,128]{2,0,1:T(8,128)(2,1)} fusion(bf16[192,512]{1,0:T(8,128)(2,1)} %param.11), kind=kLoop, calls=%fused_computation.83 | loop fusion | bytes 393216 | tf_op jit(solution)/shard_map/all_to_all | solution.py:87
  8.3 5.2 %all-to-all-start = ((bf16[192,4,128]{2,0,1:T(8,128)(2,1)}), bf16[192,4,128]{2,0,1:T(8,128)(2,1)}, u32[]{:S(2)}, u32[]{:S(2)}) async-start(bf16[192,4,128]{2,0,1:T(8,128)(2,1)} %copy_bitcast_fusion), calls=%async_computation | async-start | bytes 393216 | tf_op jit(solution)/shard_map/all_to_all | solution.py:87
  17.3 1.5 all-to-all-done
  18.8 2.6 %fusion.45 = f32[128,2304]{1,0:T(8,128)} fusion(bf16[768,128]{1,0:T(8,128)(2,1)} %bitcast.12, bf16[768,2304]{1,0:T(8,128)(2,1)S(1)} %copy-done), kind=kOutput, calls=%fused_computation.53 | convolution fusion | flops 453574656 | bytes 4915200 | tf_op jit(solution)/shard_map/dot_general | solution.py:88
  21.4 2.7 %copy.50 = f32[128,2304]{0,1:T(8,128)} copy(f32[128,2304]{1,0:T(8,128)} %fusion.45) | data formatting | bytes 2359296 | tf_op jit(solution)/shard_map/reshape | solution.py:42
  24.1 2.3 %multiply_reduce_fusion.1 = (f32[128,6]{0,1:T(8,128)S(1)}, f32[128,6]{0,1:T(8,128)S(1)}, f32[128,1,6,128]{0,3,2,1:T(8,128)}, f32[128,1,6,128]{0,3,2,1:T(8,128)}, f32[128,1,6,128]{0,3,2,1:T(8,128)}) fusion(f32[128,3,6,128]{0,3,2,1:T(8,128)} %bitcast.151), kind=kLoop, calls=%fused_computation.80 | loop fusion | flops 391680 | bytes 2365440 | tf_op jit(solution)/shard_map/reduce_sum | solution.py:46
  28.3 1.9 %copy.51 = f32[128,1,6,128]{3,0,2,1:T(8,128)} copy(f32[128,1,6,128]{0,3,2,1:T(8,128)} %get-tuple-element.311) | data formatting | bytes 786432 | tf_op jit(solution)/shard_map/slice | solution.py:44
  30.2 1.9 %copy.55 = f32[128,1,6,128]{3,0,2,1:T(8,128)} copy(f32[128,1,6,128]{0,3,2,1:T(8,128)} %get-tuple-element.310) | data formatting | bytes 786432 | tf_op jit(solution)/shard_map/slice | solution.py:45
  32.2 1.7 fusion.50
  46.0 1.9 %copy.57 = f32[128,1,6,128]{3,0,2,1:T(8,128)} copy(f32[128,1,6,128]{0,3,2,1:T(8,128)} %get-tuple-element.309) | data formatting | bytes 786432 | tf_op jit(solution)/shard_map/slice | solution.py:43
  52.3 16.6 %while.38 = (s32[]{:T(128)}, f32[6,128,256]{2,1,0:T(8,128)}, f32[2,6,64,128]{3,2,1,0:T(8,128)}, f32[2,6,64,128]{3,2,1,0:T(8,128)}, f32[2,6,64,128]{3,2,1,0:T(8,1...) while((s32[]{:T(128)}, f32[6,128,256]{2,1,0:T(8,128)}, ...), condition=%wide.region_3.4_spmd, body=%wide.region_2.3_spmd.sunk | while | flops 415678464 | bytes 10029241 | solution.py:116
  52.3 1.9 %fusion.138 = f32[6,64,256]{2,1,0:T(8,128)S(1)} fusion(f32[6,128,256]{2,1,0:T(8,128)} %get-tuple-element.456, f32[2,6,64,128]{3,2,1,0:T(8,128)} %get-tuple-element.468, s32[]{:T(128)} %get-tuple-element.455), kind=kOutput, calls=%fused_computation.13.clone.1 | convolution fusion | flops 150994944 | bytes 1376768 | tf_op jit(solution)/shard_map/while/body/eval_jaxpr/rnf,rfw->rnw/dot_general | solution.py:101
  56.7 2.9 %convolution_add_fusion.10 = f32[6,128,256]{2,1,0:T(8,128)} fusion(f32[6,128,256]{2,1,0:T(8,128)} %get-tuple-element.456, f32[6,64,128]{2,1,0:T(8,128)S(1)} %get-tuple-element.432, f32[6,64,128]{2,1,0:T(8,128)S(1)} %get-tuple-element.433, f32[2,6,64,128]{3,2,1,0:T(8,128)S(1)} %copy-done.3, s32[]{:T(128)} %get-tuple-element.455), kind=kOutput, calls=%fused_computation.clone.1 | convolution fusion | flops 151289856 | bytes 2162692 | tf_op jit(solution)/shard_map/while/body/eval_jaxpr/mjr,mjz->mrz/dot_general | solution.py:110
  60.6 1.9 %fusion.138 = f32[6,64,256]{2,1,0:T(8,128)S(1)} fusion(f32[6,128,256]{2,1,0:T(8,128)} %get-tuple-element.456, f32[2,6,64,128]{3,2,1,0:T(8,128)} %get-tuple-element.468, s32[]{:T(128)} %get-tuple-element.455), kind=kOutput, calls=%fused_computation.13.clone.1 | convolution fusion | flops 150994944 | bytes 1376768 | tf_op jit(solution)/shard_map/while/body/eval_jaxpr/rnf,rfw->rnw/dot_general | solution.py:101
  65.0 2.9 %convolution_add_fusion.10 = f32[6,128,256]{2,1,0:T(8,128)} fusion(f32[6,128,256]{2,1,0:T(8,128)} %get-tuple-element.456, f32[6,64,128]{2,1,0:T(8,128)S(1)} %get-tuple-element.432, f32[6,64,128]{2,1,0:T(8,128)S(1)} %get-tuple-element.433, f32[2,6,64,128]{3,2,1,0:T(8,128)S(1)} %copy-done.3, s32[]{:T(128)} %get-tuple-element.455), kind=kOutput, calls=%fused_computation.clone.1 | convolution fusion | flops 151289856 | bytes 2162692 | tf_op jit(solution)/shard_map/while/body/eval_jaxpr/mjr,mjz->mrz/dot_general | solution.py:110
  68.9 2.1 %fusion.65 = (f32[6,128,128]{2,1,0:T(8,128)}, f32[6,128,128]{2,1,0:T(8,128)}) fusion(f32[6,128,256]{2,1,0:T(8,128)} %get-tuple-element.180), kind=kLoop, calls=%fused_computation.98 | loop fusion | bytes 1572864 | tf_op jit(solution)/shard_map/slice | solution.py:118
  71.8 30.7 %all-gather.5.cloned.1.call-done = f32[24,128,128]{2,1,0:T(8,128)} async-done(((f32[6,128,128]{2,1,0:T(8,128)}), f32[24,128,128]{2,1,0:T(8,128)}) %all-gather.5.cloned.1.call-update) | async-done | bytes 1572880 | tf_op jit(solution)/shard_map/all_gather | solution.py:14
  102.4 32.7 %all-gather.7.cloned.1.call-done = f32[24,128,128]{2,1,0:T(8,128)} async-done(((f32[6,128,128]{2,1,0:T(8,128)}), f32[24,128,128]{2,1,0:T(8,128)}) %all-gather.7.cloned.1.call-update) | async-done | bytes 1572880 | tf_op jit(solution)/shard_map/all_gather | solution.py:14
  135.1 10.2 %while.40 = (s32[]{:T(128)}, f32[6,128,128]{2,1,0:T(8,128)}, s32[]{:T(128)}, f32[4,6,128,128]{3,2,1,0:T(8,128)}, f32[4,6,128,128]{3,2,1,0:T(8,128)}, /*index=5*/s32[]{:T(128)}, s32[]{:T(128)}) while((s32[]{:T(128)}, f32[6,128,128]{2,1,0:T(8,128)}, s32[]{:T(128)}, f32[4,6,128,128]{3,2,1,0:T(8,128)}, f32[4,6,128,128]{3,2,1,0:T(8,128)}, ...), condition=%wide.region_5.6_spmd.clone, body=%wide.region_4.5_spmd.clone.sunk | while | flops 151388160 | bytes 2755167 | solution.py:23
  136.1 2.4 %fusion.154 = f32[6,128,128]{2,1,0:T(8,128)} fusion(f32[6,128,128]{2,1,0:T(8,128)S(1)} %copy.105, f32[4,6,128,128]{3,2,1,0:T(8,128)} %get-tuple-element.491, s32[]{:T(128)} %get-tuple-element.480, f32[4,6,128,128]{3,2,1,0:T(8,128)} %get-tuple-element.490, pred[]{:T(512)S(6)} %compare.4, pred[]{:T(512)S(6)} %lt.30), kind=kOutput, calls=%fused_computation.44.clone.1 | convolution fusion | flops 151388160 | bytes 1968640 | tf_op jit(solution)/shard_map/while/body/eval_jaxpr/hij,hjk->hik/dot_general | solution.py:80
  139.5 2.4 %fusion.154 = f32[6,128,128]{2,1,0:T(8,128)} fusion(f32[6,128,128]{2,1,0:T(8,128)S(1)} %copy.105, f32[4,6,128,128]{3,2,1,0:T(8,128)} %get-tuple-element.491, s32[]{:T(128)} %get-tuple-element.480, f32[4,6,128,128]{3,2,1,0:T(8,128)} %get-tuple-element.490, pred[]{:T(512)S(6)} %compare.4, pred[]{:T(512)S(6)} %lt.30), kind=kOutput, calls=%fused_computation.44.clone.1 | convolution fusion | flops 151388160 | bytes 1968640 | tf_op jit(solution)/shard_map/while/body/eval_jaxpr/hij,hjk->hik/dot_general | solution.py:80
  142.9 2.4 %fusion.154 = f32[6,128,128]{2,1,0:T(8,128)} fusion(f32[6,128,128]{2,1,0:T(8,128)S(1)} %copy.105, f32[4,6,128,128]{3,2,1,0:T(8,128)} %get-tuple-element.491, s32[]{:T(128)} %get-tuple-element.480, f32[4,6,128,128]{3,2,1,0:T(8,128)} %get-tuple-element.490, pred[]{:T(512)S(6)} %compare.4, pred[]{:T(512)S(6)} %lt.30), kind=kOutput, calls=%fused_computation.44.clone.1 | convolution fusion | flops 151388160 | bytes 1968640 | tf_op jit(solution)/shard_map/while/body/eval_jaxpr/hij,hjk->hik/dot_general | solution.py:80
  146.1 13.8 %while.39 = (s32[]{:T(128)}, f32[6,128,128]{2,1,0:T(8,128)}, f32[2,6,64,128]{3,2,1,0:T(8,128)}, f32[2,6,64,128]{3,2,1,0:T(8,128)}, f32[2,6,64,128]{3,2,1,0:T(8,1...) while((s32[]{:T(128)}, f32[6,128,128]{2,1,0:T(8,128)}, ...), condition=%wide.region_7.8_spmd, body=%wide.region_6.7_spmd.sunk | while | flops 264388608 | bytes 9046217 | solution.py:135
  146.1 1.6 fusion.149
  147.8 1.6 fusion.150
  150.5 2.6 %convolution_subtract_fusion.3 = f32[6,128,128]{2,1,0:T(8,128)} fusion(f32[6,128,128]{2,1,0:T(8,128)} %get-tuple-element.503, f32[6,64,128]{2,1,0:T(8,128)S(1)} %fusion.149, f32[2,6,64,128]{3,2,1,0:T(8,128)S(1)} %copy-done.4, s32[]{:T(128)} %get-tuple-element.502), kind=kOutput, calls=%fused_computation.25.clone.1 | convolution fusion | flops 75595776 | bytes 1179652 | tf_op jit(solution)/shard_map/while/body/eval_jaxpr/mjr,mjz->mrz/dot_general | solution.py:130
  153.0 1.6 fusion.149
  154.7 1.6 fusion.150
  157.4 2.6 %convolution_subtract_fusion.3 = f32[6,128,128]{2,1,0:T(8,128)} fusion(f32[6,128,128]{2,1,0:T(8,128)} %get-tuple-element.503, f32[6,64,128]{2,1,0:T(8,128)S(1)} %fusion.149, f32[2,6,64,128]{3,2,1,0:T(8,128)S(1)} %copy-done.4, s32[]{:T(128)} %get-tuple-element.502), kind=kOutput, calls=%fused_computation.25.clone.1 | convolution fusion | flops 75595776 | bytes 1179652 | tf_op jit(solution)/shard_map/while/body/eval_jaxpr/mjr,mjz->mrz/dot_general | solution.py:130
  160.0 1.9 %multiply_reduce_fusion = (f32[2,64,6]{1,2,0:T(8,128)S(1)}, f32[2,64,6,128]{3,1,2,0:T(8,128)}) fusion(f32[2,6,64,128]{3,2,1,0:T(8,128)} %get-tuple-element.179, f32[2,6,64,128]{3,2,1,0:T(8,128)} %get-tuple-element.182), kind=kLoop, calls=%fused_computation.77 | loop fusion | flops 294144 | bytes 1182720 | tf_op jit(solution)/shard_map/reduce_sum | solution.py:70
  162.8 1.9 %copy.63 = f32[128,768]{1,0:T(8,128)} copy(f32[128,768]{0,1:T(8,128)} %bitcast.156) | data formatting | bytes 786432 | tf_op jit(solution)/shard_map/mul | solution.py:71
  165.9 1.8 %fusion.56 = bf16[128,768]{1,0:T(8,128)(2,1)} fusion(f32[128,768]{1,0:T(8,128)} %copy.63, f32[16,8,6,128]{3,2,1,0:T(8,128)S(1)} %bitcast.154, f32[768]{0:T(1024)S(1)} %copy-done.12), kind=kLoop, calls=%fused_computation.73 | loop fusion | flops 294912 | bytes 986112 | tf_op jit(solution)/shard_map/convert_element_type | solution.py:72
  (93 shorter events, 37.9 us)
Async XLA Ops:
  6.5 12.3 %copy-start = (bf16[768,2304]{1,0:T(8,128)(2,1)S(1)}, bf16[768,2304]{1,0:T(8,128)(2,1)}, u32[]{:S(2)}) copy-start(bf16[768,2304]{1,0:T(8,128)(2,1)} %param.12) | copy-start | bytes 10616836
  8.3 10.5 %all-to-all-start = ((bf16[192,4,128]{2,0,1:T(8,128)(2,1)}), bf16[192,4,128]{2,0,1:T(8,128)(2,1)}, u32[]{:S(2)}, u32[]{:S(2)}) async-start(bf16[192,4,128]{2,0,1:T(8,128)(2,1)} %copy_bitcast_fusion), calls=%async_computation | async-start | bytes 393216 | tf_op jit(solution)/shard_map/all_to_all | solution.py:87
  13.5 88.9 %all-gather.5.cloned.1.call-start = ((), (), s32[]{:S(2)}) async-start(), calls=%async_computation.1 | async-start | bytes 1966080 | tf_op jit(solution)/shard_map/all_gather | solution.py:14
  35.2 2.1 %copy-start.11 = (pred[64,64]{1,0:T(8,128)(4,1)S(1)}, pred[64,64]{1,0:T(8,128)(4,1)}, u32[]{:S(2)}) copy-start(pred[64,64]{1,0:T(8,128)(4,1)} %iota_compare_fusion.2) | copy-start | bytes 12292
  37.3 1.9 %copy-start.1 = (f32[2,6,64,128]{3,2,1,0:T(8,128)}, f32[2,6,64,128]{3,2,1,0:T(8,128)S(1)}, u32[]{:S(2)}) copy-start(f32[2,6,64,128]{3,2,1,0:T(8,128)S(1)} %get-tuple-element.497) | copy-start | bytes 1179652
  37.3 1.9 %copy-start.10 = (f32[64,64]{1,0:T(8,128)S(1)}, f32[64,64]{1,0:T(8,128)}, u32[]{:S(2)}) copy-start(f32[64,64]{1,0:T(8,128)} %fusion.61) | copy-start | bytes 49156
  48.0 2.0 %copy-start.2 = (f32[2,6,64,128]{3,2,1,0:T(8,128)S(1)}, f32[2,6,64,128]{3,2,1,0:T(8,128)}, u32[]{:S(2)}) copy-start(f32[2,6,64,128]{3,2,1,0:T(8,128)} %copy-done.1) | copy-start | bytes 1179652
  52.3 2.9 %copy-start.5 = (f32[2,6,64,128]{3,2,1,0:T(8,128)S(1)}, f32[2,6,64,128]{3,2,1,0:T(8,128)}, u32[]{:S(2)}) copy-start(f32[2,6,64,128]{3,2,1,0:T(8,128)} %get-tuple-element.470) | copy-start | bytes 1179652 | tf_op jit(solution)/shard_map/while
  52.3 4.4 %copy-start.3 = (f32[2,6,64,128]{3,2,1,0:T(8,128)S(1)}, f32[2,6,64,128]{3,2,1,0:T(8,128)}, u32[]{:S(2)}) copy-start(f32[2,6,64,128]{3,2,1,0:T(8,128)} %get-tuple-element.467) | copy-start | bytes 1179652 | tf_op jit(solution)/shard_map/while
  55.1 4.4 %copy-start.6 = (f32[2,6,64,64]{3,2,1,0:T(8,128)S(1)}, f32[2,6,64,64]{3,2,1,0:T(8,128)}, u32[]{:S(2)}) copy-start(f32[2,6,64,64]{3,2,1,0:T(8,128)} %get-tuple-element.471) | copy-start | bytes 589828 | tf_op jit(solution)/shard_map/while
  60.6 2.9 %copy-start.5 = (f32[2,6,64,128]{3,2,1,0:T(8,128)S(1)}, f32[2,6,64,128]{3,2,1,0:T(8,128)}, u32[]{:S(2)}) copy-start(f32[2,6,64,128]{3,2,1,0:T(8,128)} %get-tuple-element.470) | copy-start | bytes 1179652 | tf_op jit(solution)/shard_map/while
  60.6 4.4 %copy-start.3 = (f32[2,6,64,128]{3,2,1,0:T(8,128)S(1)}, f32[2,6,64,128]{3,2,1,0:T(8,128)}, u32[]{:S(2)}) copy-start(f32[2,6,64,128]{3,2,1,0:T(8,128)} %get-tuple-element.467) | copy-start | bytes 1179652 | tf_op jit(solution)/shard_map/while
  63.4 4.4 %copy-start.6 = (f32[2,6,64,64]{3,2,1,0:T(8,128)S(1)}, f32[2,6,64,64]{3,2,1,0:T(8,128)}, u32[]{:S(2)}) copy-start(f32[2,6,64,64]{3,2,1,0:T(8,128)} %get-tuple-element.471) | copy-start | bytes 589828 | tf_op jit(solution)/shard_map/while
  71.0 64.1 %all-gather.7.cloned.1.call-start = ((), (), s32[]{:S(2)}) async-start(), calls=%async_computation.2 | async-start | bytes 1966080 | tf_op jit(solution)/shard_map/all_gather | solution.py:14
  146.1 3.2 %copy-start.7 = (f32[2,6,64,64]{3,2,1,0:T(8,128)S(1)}, f32[2,6,64,64]{3,2,1,0:T(8,128)}, u32[]{:S(2)}) copy-start(f32[2,6,64,64]{3,2,1,0:T(8,128)} %get-tuple-element.516) | copy-start | bytes 589828 | tf_op jit(solution)/shard_map/while
  146.1 3.3 %copy-start.8 = (f32[2,6,64,128]{3,2,1,0:T(8,128)S(1)}, f32[2,6,64,128]{3,2,1,0:T(8,128)}, u32[]{:S(2)}) copy-start(f32[2,6,64,128]{3,2,1,0:T(8,128)} %get-tuple-element.504) | copy-start | bytes 1179652 | tf_op jit(solution)/shard_map/while
  146.1 4.3 %copy-start.4 = (f32[2,6,64,128]{3,2,1,0:T(8,128)S(1)}, f32[2,6,64,128]{3,2,1,0:T(8,128)}, u32[]{:S(2)}) copy-start(f32[2,6,64,128]{3,2,1,0:T(8,128)} %get-tuple-element.513) | copy-start | bytes 1179652 | tf_op jit(solution)/shard_map/while
  149.7 0.8 copy-start.9
  153.0 3.2 %copy-start.7 = (f32[2,6,64,64]{3,2,1,0:T(8,128)S(1)}, f32[2,6,64,64]{3,2,1,0:T(8,128)}, u32[]{:S(2)}) copy-start(f32[2,6,64,64]{3,2,1,0:T(8,128)} %get-tuple-element.516) | copy-start | bytes 589828 | tf_op jit(solution)/shard_map/while
  153.0 3.3 %copy-start.8 = (f32[2,6,64,128]{3,2,1,0:T(8,128)S(1)}, f32[2,6,64,128]{3,2,1,0:T(8,128)}, u32[]{:S(2)}) copy-start(f32[2,6,64,128]{3,2,1,0:T(8,128)} %get-tuple-element.504) | copy-start | bytes 1179652 | tf_op jit(solution)/shard_map/while
  153.0 4.3 %copy-start.4 = (f32[2,6,64,128]{3,2,1,0:T(8,128)S(1)}, f32[2,6,64,128]{3,2,1,0:T(8,128)}, u32[]{:S(2)}) copy-start(f32[2,6,64,128]{3,2,1,0:T(8,128)} %get-tuple-element.513) | copy-start | bytes 1179652 | tf_op jit(solution)/shard_map/while
  156.6 0.8 copy-start.9
  160.0 6.0 %copy-start.12 = (f32[768]{0:T(1024)S(1)}, f32[768]{0:T(1024)}, u32[]{:S(2)}) copy-start(f32[768]{0:T(1024)} %param.15) | copy-start | bytes 9220
Sparse Core Ops, SparseCore 0:
  71.1 31.2 all-gather.4
  104.3 30.8 all-gather.6
where the time goes:
time: 176 us; the launch traced here: 175 us
  waiting for transfers between devices  65.4 us (37%)
  matrix products  46.7 us (27%)
  local copies, waits for them, and re-layouts  30.2 us (17%)
  between operations  13.6 us (8%)
  other arithmetic  13 us (7%)
  starting transfers between devices  5.42 us (3%)
    all_gather x2, waiting for transfers between devices, entering(): pieces = jax.tree.map(lambda part: lax.all_gather(part, axis), value)  63.4 us
    dot_general x3, matrix products, compose(): jnp.einsum('hij,hjk->hik', second_move, first_offset, precision=HIGHEST_A...  7.21 us
    dot_general x2, matrix products, first_pass(): jnp.einsum('mjr,mjz->mrz', key_block, target_value, precision=HIGHEST_ACC...  5.78 us
    all_to_all x1, starting transfers between devices, body(): lax.all_to_all(feats, 'seq', split_axis=1, concat_axis=0, tiled=True)  5.19 us
    dot_general x2, matrix products, second_pass(): jnp.einsum('mjr,mjz->mrz', key_block, held_value, precision=HIGHEST_ACCUR...  5.12 us
    while x31, local copies, waits for them, and re-layouts  4.53 us
    dot_general x2, matrix products, first_pass(): jnp.einsum('rnf,rfw->rnw', weight_block, joint_matrix, precision=HIGHEST_...  3.72 us
  transfers between devices with their start and end apart: 3, of which 3 were waited for; matrix products, arithmetic and copies ran while one was open for 2% of the time, Pallas kernels for 0%

commit v1 on v0

--- a/solution.py
+++ b/solution.py
@@ -7,6 +7,17 @@
 HD = 128
 GROUP = 64
 HIGHEST_ACCURACY = lax.Precision.HIGHEST
+
+
+def split_up(x, dim, peers):
+    before, after = (x.shape[:dim], x.shape[dim + 1 :])
+    return jnp.moveaxis(x.reshape(*before, peers, -1, *after), dim, 0)
+
+
+def joined_along(blocks, dim):
+    blocks = jnp.moveaxis(blocks, 0, dim)
+    dims = blocks.shape
+    return blocks.reshape(*dims[:dim], dims[dim] * dims[dim + 1], *dims[dim + 2 :])
 
 
 def entering(value, axis, join, neutral):
@@ -84,7 +95,14 @@
 
 
 def body(feats, qkv_weight, beta_weight, beta_bias, out_gain):
-    local = lax.all_to_all(feats, "seq", split_axis=1, concat_axis=0, tiled=True)
+    length, place = (lax.axis_size("seq"), lax.axis_index("seq"))
+    parts = split_up(feats, 1, length)
+    outs = [parts[place]]
+    for step in range(1, length):
+        sent = parts[place ^ step]
+        outs.append(lax.ppermute(sent, "seq", [(i, i ^ step) for i in range(length)]))
+    parts = jnp.stack(outs)[place ^ jnp.arange(length)]
+    local = joined_along(parts, 0)
     qkv = lax.dot_general(
         local, qkv_weight, (((0,), (0,)), ((), ())), preferred_element_type=jnp.float32
     ).astype(jnp.bfloat16)

time: 176 us -> 183 us (1.040)
  local copies, waits for them, and re-layouts: 30.2 us -> 38.1 us
    all_to_all x1 -> x0, starting transfers between devices: 5.19 us -> none  [body(): lax.all_to_all(feats, 'seq', split_axis=1, concat_axis=0, tiled=True)]
    ppermute x0 -> x3, starting transfers between devices: none -> 4.49 us  [body(): lax.ppermute(sent, 'seq', [(i, i ^ step) for i in range(length)])]
    unnamed x12 -> x20, local copies, waits for them, and re-layouts: 0.02 us -> 2.8 us
    another operation x2 -> x3, local copies, waits for them, and re-layouts: 1.58 us -> 3.88 us
    gather x0 -> x1, local copies, waits for them, and re-layouts: none -> 2.16 us  [body(): parts = jnp.stack(outs)[place ^ jnp.arange(length)]]
  transfers between devices with their start and end apart: 3 -> 5, of which waited for: 3 -> 3; matrix products, arithmetic and copies ran while one was open for 2% -> 3% of each run, Pallas kernels for 0% -> 0%
where the time goes in v1:
time: 183 us; the launch traced here: 182 us
  waiting for transfers between devices  65.4 us (36%)
  matrix products  46.6 us (25%)
  local copies, waits for them, and re-layouts  38.1 us (21%)
  between operations  13.6 us (7%)
  other arithmetic  13.5 us (7%)
  starting transfers between devices  4.53 us (2%)
    all_gather x2, waiting for transfers between devices, entering(): pieces = jax.tree.map(lambda part: lax.all_gather(part, axis), value)  64.1 us
    dot_general x3, matrix products, compose(): jnp.einsum('hij,hjk->hik', second_move, first_offset, precision=HIGHEST_A...  7.19 us
    dot_general x2, matrix products, first_pass(): jnp.einsum('mjr,mjz->mrz', key_block, target_value, precision=HIGHEST_ACC...  5.77 us
    dot_general x2, matrix products, second_pass(): jnp.einsum('mjr,mjz->mrz', key_block, held_value, precision=HIGHEST_ACCUR...  5.11 us
    while x31, local copies, waits for them, and re-layouts  4.52 us
    ppermute x3, starting transfers between devices, body(): lax.ppermute(sent, 'seq', [(i, i ^ step) for i in range(length)])  4.49 us
    another operation x3, local copies, waits for them, and re-layouts  3.88 us
    dot_general x2, matrix products, first_pass(): jnp.einsum('rnf,rfw->rnw', weight_block, joint_matrix, precision=HIGHEST_...  3.72 us
  transfers between devices with their start and end apart: 5, of which 3 were waited for; matrix products, arithmetic and copies ran while one was open for 3% of the time, Pallas kernels for 0%

profile of v1, /device:TPU:0, one launch (start us, length us, event | category | flops | bytes accessed | tf_op | source)
XLA Modules:
  0.0 181.8 jit_solution(7164224820717150084)
XLA Ops:
  6.5 1.8 reshape.102
  8.3 2.3 %constant_dynamic-slice_fusion.3 = (bf16[192,1,128]{2,1,0:T(2,128)(2,1)}, bf16[192,1,128]{2,1,0:T(2,128)(2,1)S(1)}, bf16[192,1,128]{2,1,0:T(2,128)(2,1)S(1)}, bf16[192,1,128]{2,1,0:T(2,128)(2,1)S(1)}) fusion(bf16[192,4,128]{2,1,0:T(4,128)(2,1)} %reshape.102, s32[]{:T(128)S(6)} %select_n.52, s32[]{:T(128)S(6)} %select_n.55, s32[]{:T(128)S(6)} %select_n.54, ...), kind=kLoop, calls=%fused_computation.105 | loop fusion | bytes 393232 | tf_op jit(solution)/shard_map/dynamic-slice
  11.3 3.0 %collective-permute-start = (bf16[192,128]{1,0:T(8,128)(2,1)}, bf16[192,128]{1,0:T(8,128)(2,1)}, u32[]{:S(2)}, u32[]{:S(2)}) collective-permute-start(bf16[192,128]{1,0:T(8,128)(2,1)} %bitcast.123), channel_id=1, source_target_pairs={{0,8},{8,0},{16,24},{24,16},{1,9},{9,1},{17,25},{25,17},{2,10},{10... | collective-permute-start | bytes 147464 | tf_op jit(solution)/shard_map/ppermute | solution.py:103
  23.8 2.2 %gather_fusion = bf16[4,192,128]{2,1,0:T(8,128)(2,1)} fusion(bf16[4,192,128]{2,1,0:T(8,128)(2,1)} %pad_maximum_fusion, s32[1024]{0:T(1024)S(1)} %pad_clamp_fusion), kind=kCustom, calls=%fused_computation | custom fusion | bytes 393232 | tf_op jit(solution)/shard_map/gather | solution.py:104
  26.0 2.6 %fusion.45 = f32[128,2304]{1,0:T(8,128)} fusion(bf16[768,128]{1,0:T(8,128)(2,1)} %bitcast.169, bf16[768,2304]{1,0:T(8,128)(2,1)S(1)} %copy-done), kind=kOutput, calls=%fused_computation.54 | convolution fusion | flops 453574656 | bytes 4915200 | tf_op jit(solution)/shard_map/dot_general | solution.py:106
  28.6 2.7 %copy.47 = f32[128,2304]{0,1:T(8,128)} copy(f32[128,2304]{1,0:T(8,128)} %fusion.45) | data formatting | bytes 2359296 | tf_op jit(solution)/shard_map/reshape | solution.py:53
  31.3 2.3 %multiply_reduce_fusion.1 = (f32[128,6]{0,1:T(8,128)S(1)}, f32[128,6]{0,1:T(8,128)S(1)}, f32[128,1,6,128]{0,3,2,1:T(8,128)}, f32[128,1,6,128]{0,3,2,1:T(8,128)}, f32[128,1,6,128]{0,3,2,1:T(8,128)}) fusion(f32[128,3,6,128]{0,3,2,1:T(8,128)} %bitcast.161), kind=kLoop, calls=%fused_computation.81 | loop fusion | flops 391680 | bytes 2365440 | tf_op jit(solution)/shard_map/reduce_sum | solution.py:57
  33.6 1.9 %copy.54 = f32[128,1,6,128]{3,0,2,1:T(8,128)} copy(f32[128,1,6,128]{0,3,2,1:T(8,128)} %get-tuple-element.309) | data formatting | bytes 786432 | tf_op jit(solution)/shard_map/slice | solution.py:54
  37.5 1.9 %copy.48 = f32[128,1,6,128]{3,0,2,1:T(8,128)} copy(f32[128,1,6,128]{0,3,2,1:T(8,128)} %get-tuple-element.311) | data formatting | bytes 786432 | tf_op jit(solution)/shard_map/slice | solution.py:55
  39.4 1.9 %copy.52 = f32[128,1,6,128]{3,0,2,1:T(8,128)} copy(f32[128,1,6,128]{0,3,2,1:T(8,128)} %get-tuple-element.310) | data formatting | bytes 786432 | tf_op jit(solution)/shard_map/slice | solution.py:56
  42.7 1.7 fusion.50
  58.9 16.6 %while.38 = (s32[]{:T(128)}, f32[6,128,256]{2,1,0:T(8,128)}, f32[2,6,64,128]{3,2,1,0:T(8,128)}, f32[2,6,64,128]{3,2,1,0:T(8,128)}, f32[2,6,64,128]{3,2,1,0:T(8,1...) while((s32[]{:T(128)}, f32[6,128,256]{2,1,0:T(8,128)}, ...), condition=%wide.region_3.4_spmd, body=%wide.region_2.3_spmd.sunk | while | flops 415678464 | bytes 10029241 | solution.py:134
  58.9 1.9 %fusion.138 = f32[6,64,256]{2,1,0:T(8,128)S(1)} fusion(f32[6,128,256]{2,1,0:T(8,128)} %get-tuple-element.460, f32[2,6,64,128]{3,2,1,0:T(8,128)} %get-tuple-element.472, s32[]{:T(128)} %get-tuple-element.459), kind=kOutput, calls=%fused_computation.14.clone.1 | convolution fusion | flops 150994944 | bytes 1376768 | tf_op jit(solution)/shard_map/while/body/eval_jaxpr/rnf,rfw->rnw/dot_general | solution.py:119
  63.4 2.9 %convolution_add_fusion.10 = f32[6,128,256]{2,1,0:T(8,128)} fusion(f32[6,128,256]{2,1,0:T(8,128)} %get-tuple-element.460, f32[6,64,128]{2,1,0:T(8,128)S(1)} %get-tuple-element.436, f32[6,64,128]{2,1,0:T(8,128)S(1)} %get-tuple-element.437, f32[2,6,64,128]{3,2,1,0:T(8,128)S(1)} %copy-done.2, s32[]{:T(128)} %get-tuple-element.459), kind=kOutput, calls=%fused_computation.1.clone.1 | convolution fusion | flops 151289856 | bytes 2162692 | tf_op jit(solution)/shard_map/while/body/eval_jaxpr/mjr,mjz->mrz/dot_general | solution.py:128
  67.3 1.9 %fusion.138 = f32[6,64,256]{2,1,0:T(8,128)S(1)} fusion(f32[6,128,256]{2,1,0:T(8,128)} %get-tuple-element.460, f32[2,6,64,128]{3,2,1,0:T(8,128)} %get-tuple-element.472, s32[]{:T(128)} %get-tuple-element.459), kind=kOutput, calls=%fused_computation.14.clone.1 | convolution fusion | flops 150994944 | bytes 1376768 | tf_op jit(solution)/shard_map/while/body/eval_jaxpr/rnf,rfw->rnw/dot_general | solution.py:119
  71.7 2.9 %convolution_add_fusion.10 = f32[6,128,256]{2,1,0:T(8,128)} fusion(f32[6,128,256]{2,1,0:T(8,128)} %get-tuple-element.460, f32[6,64,128]{2,1,0:T(8,128)S(1)} %get-tuple-element.436, f32[6,64,128]{2,1,0:T(8,128)S(1)} %get-tuple-element.437, f32[2,6,64,128]{3,2,1,0:T(8,128)S(1)} %copy-done.2, s32[]{:T(128)} %get-tuple-element.459), kind=kOutput, calls=%fused_computation.1.clone.1 | convolution fusion | flops 151289856 | bytes 2162692 | tf_op jit(solution)/shard_map/while/body/eval_jaxpr/mjr,mjz->mrz/dot_general | solution.py:128
  75.5 2.1 %fusion.66 = (f32[6,128,128]{2,1,0:T(8,128)}, f32[6,128,128]{2,1,0:T(8,128)}) fusion(f32[6,128,256]{2,1,0:T(8,128)} %get-tuple-element.180), kind=kLoop, calls=%fused_computation.110 | loop fusion | bytes 1572864 | tf_op jit(solution)/shard_map/slice | solution.py:136
  78.4 31.4 %all-gather.5.cloned.1.call-done = f32[24,128,128]{2,1,0:T(8,128)} async-done(((f32[6,128,128]{2,1,0:T(8,128)}), f32[24,128,128]{2,1,0:T(8,128)}) %all-gather.5.cloned.1.call-update) | async-done | bytes 1572880 | tf_op jit(solution)/shard_map/all_gather | solution.py:25
  109.8 32.7 %all-gather.7.cloned.1.call-done = f32[24,128,128]{2,1,0:T(8,128)} async-done(((f32[6,128,128]{2,1,0:T(8,128)}), f32[24,128,128]{2,1,0:T(8,128)}) %all-gather.7.cloned.1.call-update) | async-done | bytes 1572880 | tf_op jit(solution)/shard_map/all_gather | solution.py:25
  142.5 10.2 %while.40 = (s32[]{:T(128)}, f32[6,128,128]{2,1,0:T(8,128)}, s32[]{:T(128)}, f32[4,6,128,128]{3,2,1,0:T(8,128)}, f32[4,6,128,128]{3,2,1,0:T(8,128)}, /*index=5*/s32[]{:T(128)}, s32[]{:T(128)}) while((s32[]{:T(128)}, f32[6,128,128]{2,1,0:T(8,128)}, s32[]{:T(128)}, f32[4,6,128,128]{3,2,1,0:T(8,128)}, f32[4,6,128,128]{3,2,1,0:T(8,128)}, ...), condition=%wide.region_5.6_spmd.clone, body=%wide.region_4.5_spmd.clone.sunk | while | flops 151388160 | bytes 2755167 | solution.py:34
  143.5 2.4 %fusion.154 = f32[6,128,128]{2,1,0:T(8,128)} fusion(f32[6,128,128]{2,1,0:T(8,128)S(1)} %copy.112, f32[4,6,128,128]{3,2,1,0:T(8,128)} %get-tuple-element.495, s32[]{:T(128)} %get-tuple-element.484, f32[4,6,128,128]{3,2,1,0:T(8,128)} %get-tuple-element.494, pred[]{:T(512)S(6)} %compare.4, pred[]{:T(512)S(6)} %lt.60), kind=kOutput, calls=%fused_computation.45.clone.1 | convolution fusion | flops 151388160 | bytes 1968640 | tf_op jit(solution)/shard_map/while/body/eval_jaxpr/hij,hjk->hik/dot_general | solution.py:91
  146.9 2.4 %fusion.154 = f32[6,128,128]{2,1,0:T(8,128)} fusion(f32[6,128,128]{2,1,0:T(8,128)S(1)} %copy.112, f32[4,6,128,128]{3,2,1,0:T(8,128)} %get-tuple-element.495, s32[]{:T(128)} %get-tuple-element.484, f32[4,6,128,128]{3,2,1,0:T(8,128)} %get-tuple-element.494, pred[]{:T(512)S(6)} %compare.4, pred[]{:T(512)S(6)} %lt.60), kind=kOutput, calls=%fused_computation.45.clone.1 | convolution fusion | flops 151388160 | bytes 1968640 | tf_op jit(solution)/shard_map/while/body/eval_jaxpr/hij,hjk->hik/dot_general | solution.py:91
  150.3 2.4 %fusion.154 = f32[6,128,128]{2,1,0:T(8,128)} fusion(f32[6,128,128]{2,1,0:T(8,128)S(1)} %copy.112, f32[4,6,128,128]{3,2,1,0:T(8,128)} %get-tuple-element.495, s32[]{:T(128)} %get-tuple-element.484, f32[4,6,128,128]{3,2,1,0:T(8,128)} %get-tuple-element.494, pred[]{:T(512)S(6)} %compare.4, pred[]{:T(512)S(6)} %lt.60), kind=kOutput, calls=%fused_computation.45.clone.1 | convolution fusion | flops 151388160 | bytes 1968640 | tf_op jit(solution)/shard_map/while/body/eval_jaxpr/hij,hjk->hik/dot_general | solution.py:91
  153.5 13.8 %while.39 = (s32[]{:T(128)}, f32[6,128,128]{2,1,0:T(8,128)}, f32[2,6,64,128]{3,2,1,0:T(8,128)}, f32[2,6,64,128]{3,2,1,0:T(8,128)}, f32[2,6,64,128]{3,2,1,0:T(8,1...) while((s32[]{:T(128)}, f32[6,128,128]{2,1,0:T(8,128)}, ...), condition=%wide.region_7.8_spmd, body=%wide.region_6.7_spmd.sunk | while | flops 264388608 | bytes 9046217 | solution.py:153
  153.5 1.6 fusion.149
  155.1 1.6 fusion.150
  157.8 2.6 %convolution_subtract_fusion.3 = f32[6,128,128]{2,1,0:T(8,128)} fusion(f32[6,128,128]{2,1,0:T(8,128)} %get-tuple-element.507, f32[6,64,128]{2,1,0:T(8,128)S(1)} %fusion.149, f32[2,6,64,128]{3,2,1,0:T(8,128)S(1)} %copy-done.3, s32[]{:T(128)} %get-tuple-element.506), kind=kOutput, calls=%fused_computation.26.clone.1 | convolution fusion | flops 75595776 | bytes 1179652 | tf_op jit(solution)/shard_map/while/body/eval_jaxpr/mjr,mjz->mrz/dot_general | solution.py:148
  160.4 1.6 fusion.149
  164.7 2.6 %convolution_subtract_fusion.3 = f32[6,128,128]{2,1,0:T(8,128)} fusion(f32[6,128,128]{2,1,0:T(8,128)} %get-tuple-element.507, f32[6,64,128]{2,1,0:T(8,128)S(1)} %fusion.149, f32[2,6,64,128]{3,2,1,0:T(8,128)S(1)} %copy-done.3, s32[]{:T(128)} %get-tuple-element.506), kind=kOutput, calls=%fused_computation.26.clone.1 | convolution fusion | flops 75595776 | bytes 1179652 | tf_op jit(solution)/shard_map/while/body/eval_jaxpr/mjr,mjz->mrz/dot_general | solution.py:148
  167.3 1.9 %multiply_reduce_fusion = (f32[2,64,6]{1,2,0:T(8,128)S(1)}, f32[2,64,6,128]{3,1,2,0:T(8,128)}) fusion(f32[2,6,64,128]{3,2,1,0:T(8,128)} %get-tuple-element.179, f32[2,6,64,128]{3,2,1,0:T(8,128)} %get-tuple-element.182), kind=kLoop, calls=%fused_computation.78 | loop fusion | flops 294144 | bytes 1182720 | tf_op jit(solution)/shard_map/reduce_sum | solution.py:81
  170.1 1.9 %copy.60 = f32[128,768]{1,0:T(8,128)} copy(f32[128,768]{0,1:T(8,128)} %bitcast.166) | data formatting | bytes 786432 | tf_op jit(solution)/shard_map/mul | solution.py:82
  173.2 1.8 fusion.56
  (110 shorter events, 45.4 us)
Async XLA Ops:
  6.5 19.5 %copy-start = (bf16[768,2304]{1,0:T(8,128)(2,1)S(1)}, bf16[768,2304]{1,0:T(8,128)(2,1)}, u32[]{:S(2)}) copy-start(bf16[768,2304]{1,0:T(8,128)(2,1)} %param.12) | copy-start | bytes 10616836
  6.5 103.2 %all-gather.5.cloned.1.call-start = ((), (), s32[]{:S(2)}) async-start(), calls=%async_computation | async-start | bytes 1966080 | tf_op jit(solution)/shard_map/all_gather | solution.py:25
  11.3 10.4 %collective-permute-start = (bf16[192,128]{1,0:T(8,128)(2,1)}, bf16[192,128]{1,0:T(8,128)(2,1)}, u32[]{:S(2)}, u32[]{:S(2)}) collective-permute-start(bf16[192,128]{1,0:T(8,128)(2,1)} %bitcast.123), channel_id=1, source_target_pairs={{0,8},{8,0},{16,24},{24,16},{1,9},{9,1},{17,25},{25,17},{2,10},{10... | collective-permute-start | bytes 147464 | tf_op jit(solution)/shard_map/ppermute | solution.py:103
  14.8 6.8 %collective-permute-start.1 = (bf16[192,128]{1,0:T(8,128)(2,1)}, bf16[192,128]{1,0:T(8,128)(2,1)}, u32[]{:S(2)}, u32[]{:S(2)}) collective-permute-start(bf16[192,128]{1,0:T(8,128)(2,1)} %bitcast.122), channel_id=1, source_target_pairs={{0,16},{8,24},{16,0},{24,8},{1,17},{9,25},{17,1},{25,9},{2,18},{10... | collective-permute-start | bytes 147464 | tf_op jit(solution)/shard_map/ppermute | solution.py:103
  17.0 5.3 %collective-permute-start.2 = (bf16[192,128]{1,0:T(8,128)(2,1)}, bf16[192,128]{1,0:T(8,128)(2,1)}, u32[]{:S(2)}, u32[]{:S(2)}) collective-permute-start(bf16[192,128]{1,0:T(8,128)(2,1)} %bitcast.121), channel_id=1, source_target_pairs={{0,24},{8,16},{16,8},{24,0},{1,25},{9,17},{17,9},{25,1},{2,26},{10... | collective-permute-start | bytes 147464 | tf_op jit(solution)/shard_map/ppermute | solution.py:103
  36.1 5.2 %copy-start.13 = (f32[128,6]{0,1:T(8,128)S(1)}, f32[128,6]{0,1:T(8,128)}, u32[]{:S(2)}) copy-start(f32[128,6]{0,1:T(8,128)} %get-tuple-element.322) | copy-start | bytes 9220
  45.7 2.7 %copy-start.9 = (f32[128,1,6,128]{3,0,2,1:T(8,128)S(1)}, f32[128,1,6,128]{3,0,2,1:T(8,128)}, u32[]{:S(2)}) copy-start(f32[128,1,6,128]{3,0,2,1:T(8,128)} %copy.48) | copy-start | bytes 1179652
  45.7 2.7 %copy-start.10 = (f32[128,1,6,128]{3,0,2,1:T(8,128)S(1)}, f32[128,1,6,128]{3,0,2,1:T(8,128)}, u32[]{:S(2)}) copy-start(f32[128,1,6,128]{3,0,2,1:T(8,128)} %copy.52) | copy-start | bytes 1179652
  48.4 1.8 copy-start.12
  48.7 2.8 %copy-start.1 = (f32[2,6,64,128]{3,2,1,0:T(8,128)}, f32[2,6,64,128]{3,2,1,0:T(8,128)S(1)}, u32[]{:S(2)}) copy-start(f32[2,6,64,128]{3,2,1,0:T(8,128)S(1)} %get-tuple-element.501) | copy-start | bytes 1179652
  50.2 1.9 %copy-start.11 = (f32[64,64]{1,0:T(8,128)S(1)}, f32[64,64]{1,0:T(8,128)}, u32[]{:S(2)}) copy-start(f32[64,64]{1,0:T(8,128)} %fusion.61) | copy-start | bytes 49156
  58.9 2.9 %copy-start.4 = (f32[2,6,64,128]{3,2,1,0:T(8,128)S(1)}, f32[2,6,64,128]{3,2,1,0:T(8,128)}, u32[]{:S(2)}) copy-start(f32[2,6,64,128]{3,2,1,0:T(8,128)} %get-tuple-element.474) | copy-start | bytes 1179652 | tf_op jit(solution)/shard_map/while
  58.9 4.4 %copy-start.2 = (f32[2,6,64,128]{3,2,1,0:T(8,128)S(1)}, f32[2,6,64,128]{3,2,1,0:T(8,128)}, u32[]{:S(2)}) copy-start(f32[2,6,64,128]{3,2,1,0:T(8,128)} %get-tuple-element.471) | copy-start | bytes 1179652 | tf_op jit(solution)/shard_map/while
  61.8 4.4 %copy-start.5 = (f32[2,6,64,64]{3,2,1,0:T(8,128)S(1)}, f32[2,6,64,64]{3,2,1,0:T(8,128)}, u32[]{:S(2)}) copy-start(f32[2,6,64,64]{3,2,1,0:T(8,128)} %get-tuple-element.475) | copy-start | bytes 589828 | tf_op jit(solution)/shard_map/while
  67.2 2.9 %copy-start.4 = (f32[2,6,64,128]{3,2,1,0:T(8,128)S(1)}, f32[2,6,64,128]{3,2,1,0:T(8,128)}, u32[]{:S(2)}) copy-start(f32[2,6,64,128]{3,2,1,0:T(8,128)} %get-tuple-element.474) | copy-start | bytes 1179652 | tf_op jit(solution)/shard_map/while
  67.2 4.4 %copy-start.2 = (f32[2,6,64,128]{3,2,1,0:T(8,128)S(1)}, f32[2,6,64,128]{3,2,1,0:T(8,128)}, u32[]{:S(2)}) copy-start(f32[2,6,64,128]{3,2,1,0:T(8,128)} %get-tuple-element.471) | copy-start | bytes 1179652 | tf_op jit(solution)/shard_map/while
  70.1 4.4 %copy-start.5 = (f32[2,6,64,64]{3,2,1,0:T(8,128)S(1)}, f32[2,6,64,64]{3,2,1,0:T(8,128)}, u32[]{:S(2)}) copy-start(f32[2,6,64,64]{3,2,1,0:T(8,128)} %get-tuple-element.475) | copy-start | bytes 589828 | tf_op jit(solution)/shard_map/while
  77.7 64.8 %all-gather.7.cloned.1.call-start = ((), (), s32[]{:S(2)}) async-start(), calls=%async_computation.1 | async-start | bytes 1966080 | tf_op jit(solution)/shard_map/all_gather | solution.py:25
  153.5 3.2 %copy-start.6 = (f32[2,6,64,64]{3,2,1,0:T(8,128)S(1)}, f32[2,6,64,64]{3,2,1,0:T(8,128)}, u32[]{:S(2)}) copy-start(f32[2,6,64,64]{3,2,1,0:T(8,128)} %get-tuple-element.520) | copy-start | bytes 589828 | tf_op jit(solution)/shard_map/while
  153.5 3.3 %copy-start.7 = (f32[2,6,64,128]{3,2,1,0:T(8,128)S(1)}, f32[2,6,64,128]{3,2,1,0:T(8,128)}, u32[]{:S(2)}) copy-start(f32[2,6,64,128]{3,2,1,0:T(8,128)} %get-tuple-element.508) | copy-start | bytes 1179652 | tf_op jit(solution)/shard_map/while
  153.5 4.3 %copy-start.3 = (f32[2,6,64,128]{3,2,1,0:T(8,128)S(1)}, f32[2,6,64,128]{3,2,1,0:T(8,128)}, u32[]{:S(2)}) copy-start(f32[2,6,64,128]{3,2,1,0:T(8,128)} %get-tuple-element.517) | copy-start | bytes 1179652 | tf_op jit(solution)/shard_map/while
  157.1 0.7 copy-start.8
  160.4 3.2 %copy-start.6 = (f32[2,6,64,64]{3,2,1,0:T(8,128)S(1)}, f32[2,6,64,64]{3,2,1,0:T(8,128)}, u32[]{:S(2)}) copy-start(f32[2,6,64,64]{3,2,1,0:T(8,128)} %get-tuple-element.520) | copy-start | bytes 589828 | tf_op jit(solution)/shard_map/while
  160.4 3.3 %copy-start.7 = (f32[2,6,64,128]{3,2,1,0:T(8,128)S(1)}, f32[2,6,64,128]{3,2,1,0:T(8,128)}, u32[]{:S(2)}) copy-start(f32[2,6,64,128]{3,2,1,0:T(8,128)} %get-tuple-element.508) | copy-start | bytes 1179652 | tf_op jit(solution)/shard_map/while
  160.4 4.3 %copy-start.3 = (f32[2,6,64,128]{3,2,1,0:T(8,128)S(1)}, f32[2,6,64,128]{3,2,1,0:T(8,128)}, u32[]{:S(2)}) copy-start(f32[2,6,64,128]{3,2,1,0:T(8,128)} %get-tuple-element.517) | copy-start | bytes 1179652 | tf_op jit(solution)/shard_map/while
  164.0 0.7 copy-start.8
  167.3 6.0 %copy-start.14 = (f32[768]{0:T(1024)S(1)}, f32[768]{0:T(1024)}, u32[]{:S(2)}) copy-start(f32[768]{0:T(1024)} %param.15) | copy-start | bytes 9220
Sparse Core Ops, SparseCore 0:
  77.8 31.9 all-gather.4
  111.6 30.8 all-gather.6
